TPU v7x, 512 devices: a whole 4x8x8 slice. The times are simulated.
512 devices in a mesh: ep: 128 (over y, z, core), dp: 4 (over x).
Axes of the slice: x: 4, y: 8, z: 8, core: 2. Of those that a mesh axis runs over, the one named last changes fastest.
Arguments:
- tokens: bfloat16 [2, 2048, 3584], P(None, ('ep', 'dp')), may hold values from -6 to 6
- routing: int32 [2, 2048, 8], P(None, 'ep'), may hold values from 0 to 127, all different within a row; in each aligned block of 16 rows (0 to 15, 16 to 31, ..., all dimensions but the last counted through in order) at most 2 rows name the same one
- gate_values: float32 [2, 2048, 8], P(None, 'ep'), may hold values from 0.05 to 0.5
- held_weight: bfloat16 [128, 3584, 1024], P('ep', None, 'dp'), may hold values from -0.09375 to 0.09375
- scale_table: float32 [128, 28, 8], P(None, None, 'dp'), may hold values from 0.25 to 4
- old_expert: int32 [128], replicated, may hold values from 0 to 127, as said below
- new_expert: int32 [128], replicated, may hold values from 0 to 127, as said below
Outputs:
- combined: bfloat16 [2, 2048, 1024], P(None, 'ep', 'dp')
- moved_weight: bfloat16 [128, 3584, 1024], P('ep', None, 'dp')
Inputs may be any that keep to these rules, and one draw needn't show every extreme that they name: `routing`: each row names 8 different experts; in each aligned block of 16 token rows of a step no expert is named by more than 2 rows. `old_expert`: A permutation of the experts over the slots. `new_expert`: A permutation of the experts over the slots; it equals old_expert except at exactly 32 slots, whose experts are permuted among themselves so that each of them changes.
All inputs are finite; a program needn't handle non-finite values.
Results may differ from a plain program's by a relative error of at most 0.0039.
Values may be sent and summed in bfloat16 or wider, within the bound.
No kernel may reach another device: no remote copies, remote signals or barrier semaphores. Data moves between devices by JAX's collectives and lax.ppermute only.
A program may use at most 64 MiB of HBM per device.

v0:
```python
import jax
import jax.numpy as jnp
from jax import lax
from jax.sharding import PartitionSpec as P


def inverse_place(expert_at):
    count = expert_at.shape[0]
    labels = jnp.arange(count, dtype=jnp.int32)
    match = expert_at[None, :] == labels[:, None]
    return jnp.sum(jnp.where(match, labels[None, :], 0), axis=1)


def source_slots(old_expert, new_expert):
    labels = jnp.arange(old_expert.shape[0], dtype=jnp.int32)
    match = old_expert[None, :] == new_expert[:, None]
    return jnp.sum(jnp.where(match, labels[None, :], 0), axis=1)


def scaled_product(token_rows, weight_block, scales):
    row_blocks = scales.shape[0]
    block_rows = weight_block.shape[0] // row_blocks
    partial_value = jnp.einsum(
        "rbi,bif->rbf",
        token_rows.reshape(token_rows.shape[0], row_blocks, block_rows),
        weight_block.reshape(row_blocks, block_rows, weight_block.shape[1]),
        preferred_element_type=jnp.float32,
    )
    widened = jnp.repeat(scales, weight_block.shape[1] // scales.shape[1], axis=1)
    return jnp.sum(partial_value * widened[None, :, :], axis=1)


def expert_service(weight_block, scales):

    def serve_rows(arrived):

        def one_slot(slot_rows):
            return jax.nn.silu(scaled_product(slot_rows, weight_block, scales)).astype(jnp.bfloat16)

        activated = lax.map(one_slot, arrived)
        return lax.all_to_all(activated, "ep", split_axis=1, concat_axis=1, tiled=True)

    return serve_rows


def route_pairs(routing, expert_at, peers):
    pair_ids = routing.reshape(-1)
    labels = jnp.arange(peers, dtype=jnp.int32)
    onehot = (pair_ids[:, None] == labels[None, :]).astype(jnp.int32)
    before = jnp.cumsum(onehot, axis=0) - onehot
    slot_rank = jnp.sum(before * onehot, axis=1)
    owners = jnp.sum(onehot * inverse_place(expert_at)[None, :], axis=1)
    return slot_rank * peers + owners


def shards(tokens, routing, gate_values, held_weight, scale_table, old_expert, new_expert):
    peers = lax.axis_size("ep")
    my_slot = lax.axis_index("ep")
    group_size = routing.shape[1]
    top_count = routing.shape[2]
    capacity = min(group_size, max(2, 2 * group_size * top_count // peers))
    hidden_width = held_weight.shape[2]
    old_block = held_weight[0]
    sources = source_slots(old_expert, new_expert)
    pieces = old_block.reshape(peers, old_block.shape[0] // peers, hidden_width)
    new_block = lax.all_to_all(
        jnp.take(
            lax.all_to_all(pieces, "ep", split_axis=0, concat_axis=0, tiled=True), sources, axis=0
        ),
        "ep",
        split_axis=0,
        concat_axis=0,
        tiled=True,
    ).reshape(old_block.shape)
    first_serve = (new_block, new_expert)
    serve_plans = [first_serve] + [(new_block, new_expert)] * (tokens.shape[0] - 1)
    grouped = lax.all_gather(tokens, "dp", axis=1, tiled=True)
    columns = grouped.shape[2]
    combined_steps = []
    for decode_step in range(tokens.shape[0]):
        weight_block, expert_at = serve_plans[decode_step]
        scales = scale_table[expert_at[my_slot]]
        target = route_pairs(routing[decode_step], expert_at, peers)
        repeated = jnp.repeat(grouped[decode_step], top_count, axis=0)
        send_buffer = jnp.zeros((capacity * peers, columns), grouped.dtype).at[target].set(repeated)
        send_buffer = send_buffer.reshape(capacity, peers, columns)
        serve_rows = expert_service(weight_block, scales)
        returned = serve_rows(
            lax.all_to_all(send_buffer, "ep", split_axis=1, concat_axis=1, tiled=True)
        )
        activated = returned.reshape(capacity * peers, hidden_width)[target].astype(jnp.float32)
        activated = activated.reshape(group_size, top_count, hidden_width)
        weighted = jnp.sum(gate_values[decode_step][:, :, None] * activated, axis=1)
        combined_steps.append(weighted.astype(jnp.bfloat16))
    return (jnp.stack(combined_steps), new_block[None])


def solution(mesh):
    placed = (
        P(None, ("ep", "dp"), None),
        P(None, "ep", None),
        P(None, "ep", None),
        P("ep", None, "dp"),
        P(None, None, "dp"),
        P(),
        P(),
    )
    return jax.shard_map(
        shards,
        mesh=mesh,
        in_specs=placed,
        out_specs=(P(None, "ep", "dp"), P("ep", None, "dp")),
        check_vma=False,
    )
```

profile of v0, /device:TPU:1, one launch (start us, length us, event | category | flops | bytes accessed | tf_op | source)
XLA Modules:
  0.0 315.5 jit_solution(4355905081281846887)
XLA Ops:
  3.1 10.5 %all_gather.3 = bf16[2,16,3584]{2,0,1:T(2,128)(2,1)S(1)} all-gather(bf16[2,4,3584]{2,0,1:T(2,128)(2,1)S(1)} %copy.58), channel_id=1, replica_groups=mesh['ep'=128,'dp'=4] {'dp'}, dimensions={1}, use_global_device_ids=true | all-gather | bytes 286720 | tf_op jit(solution)/shard_map/all_gather | solution.py:77
  17.5 3.1 copy.60
  20.7 20.5 %all-to-all-start = ((bf16[2,128,3584]{2,0,1:T(2,128)(2,1)}), bf16[2,128,3584]{2,0,1:T(2,128)(2,1)S(1)}, u32[]{:S(2)}, u32[]{:S(2)}) async-start(bf16[2,128,3584]{2,0,1:T(2,128)(2,1)} %copy.60), calls=%async_computation | async-start | bytes 3670016 | tf_op jit(solution)/shard_map/all_to_all | solution.py:89
  41.1 3.7 %reshape_squeeze.3 = bf16[128,28,256]{2,1,0:T(8,128)(2,1)} reshape(bf16[1,3584,256]{2,1,0:T(8,128)(2,1)} %param.14) | data formatting | bytes 3670016 | tf_op jit(solution)/shard_map/reshape;squeeze | solution.py:65
  44.9 42.7 %all-to-all-done = bf16[2,128,3584]{2,0,1:T(2,128)(2,1)S(1)} async-done(((bf16[2,128,3584]{2,0,1:T(2,128)(2,1)}), bf16[2,128,3584]{2,0,1:T(2,128)(2,1)S(1)}, u32[]{:S(2)}, u32[]{:S(2)}) %all-to-all-start) | async-done | bytes 1835040 | tf_op jit(solution)/shard_map/all_to_all | solution.py:89
  88.9 7.8 %all-to-all-start.1 = ((bf16[128,28,256]{2,1,0:T(8,128)(2,1)}), bf16[128,28,256]{2,1,0:T(8,128)(2,1)S(1)}, u32[]{:S(2)}, u32[]{:S(2)}) async-start(bf16[128,28,256]{2,1,0:T(8,128)(2,1)} %reshape_squeeze.3), calls=%async_computation.1 | async-start | bytes 4194304 | tf_op jit(solution)/shard_map/all_to_all | solution.py:68
  96.7 3.3 %scatter_custom_fusion.1 = bf16[256,3584]{1,0:T(8,128)(2,1)} fusion(s32[128]{0:T(128)S(1)} %get-tuple-element.141, bf16[]{:T(256)} %constant.58.clone.1, bf16[16,3584]{1,0:T(8,128)(2,1)S(1)} %get-tuple-element.142), kind=kCustom, calls=%fused_computation.24 | custom fusion | bytes 1949698 | tf_op jit(solution)/shard_map/scatter | solution.py:85
  100.0 4.6 %copy.69 = bf16[2,128,3584]{2,0,1:T(2,128)(2,1)} copy(bf16[2,128,3584]{2,1,0:T(8,128)(2,1)} %bitcast.125) | data formatting | bytes 3670016 | tf_op jit(solution)/shard_map/reshape | solution.py:86
  104.6 44.2 %all-to-all-done.1 = bf16[128,28,256]{2,1,0:T(8,128)(2,1)S(1)} async-done(((bf16[128,28,256]{2,1,0:T(8,128)(2,1)}), bf16[128,28,256]{2,1,0:T(8,128)(2,1)S(1)}, u32[]{:S(2)}, u32[]{:S(2)}) %all-to-all-start.1) | async-done | bytes 1835040 | tf_op jit(solution)/shard_map/all_to_all | solution.py:68
  148.8 8.1 %all-to-all-start.4 = ((bf16[2,128,3584]{2,0,1:T(2,128)(2,1)}), bf16[2,128,3584]{2,0,1:T(2,128)(2,1)}, u32[]{:S(2)}, u32[]{:S(2)}) async-start(bf16[2,128,3584]{2,0,1:T(2,128)(2,1)} %copy.69), calls=%async_computation.4 | async-start | bytes 3670016 | tf_op jit(solution)/shard_map/all_to_all | solution.py:89
  159.0 3.2 %broadcast_select_fusion = bf16[128,28,256]{2,1,0:T(8,128)(2,1)} fusion(bf16[128,28,256]{2,1,0:T(8,128)(2,1)} %gather_fusion, pred[128]{0:T(512)(128)(4,1)S(1)} %compare_and_fusion), kind=kLoop, calls=%fused_computation.23 | loop fusion | flops 917504 | bytes 3670144 | tf_op jit(solution)/shard_map/jit(_take)/select_n | solution.py:67
  162.2 40.9 %all-to-all-done.4 = bf16[2,128,3584]{2,0,1:T(2,128)(2,1)} async-done(((bf16[2,128,3584]{2,0,1:T(2,128)(2,1)}), bf16[2,128,3584]{2,0,1:T(2,128)(2,1)}, u32[]{:S(2)}, u32[]{:S(2)}) %all-to-all-start.4) | async-done | bytes 1835040 | tf_op jit(solution)/shard_map/all_to_all | solution.py:89
  203.1 7.8 %all-to-all-start.2 = ((bf16[128,28,256]{2,1,0:T(8,128)(2,1)}), bf16[128,28,256]{2,1,0:T(8,128)(2,1)S(1)}, u32[]{:S(2)}, u32[]{:S(2)}) async-start(bf16[128,28,256]{2,1,0:T(8,128)(2,1)} %broadcast_select_fusion), calls=%async_computation.2 | async-start | bytes 4194304 | tf_op jit(solution)/shard_map/all_to_all | solution.py:66
  213.8 5.6 %copy.62 = bf16[2,128,3584]{1,2,0:T(8,128)(2,1)} copy(bf16[2,128,3584]{2,0,1:T(2,128)(2,1)} %copy-done.3) | data formatting | bytes 3670016 | tf_op jit(solution)/shard_map/while | solution.py:40
  219.3 5.5 %copy.70 = bf16[2,128,3584]{1,2,0:T(8,128)(2,1)} copy(bf16[2,128,3584]{2,0,1:T(2,128)(2,1)} %all-to-all-done.4) | data formatting | bytes 3670016 | tf_op jit(solution)/shard_map/while | solution.py:40
  224.9 38.2 %all-to-all-done.2 = bf16[128,28,256]{2,1,0:T(8,128)(2,1)S(1)} async-done(((bf16[128,28,256]{2,1,0:T(8,128)(2,1)}), bf16[128,28,256]{2,1,0:T(8,128)(2,1)S(1)}, u32[]{:S(2)}, u32[]{:S(2)}) %all-to-all-start.2) | async-done | bytes 1835040 | tf_op jit(solution)/shard_map/all_to_all | solution.py:66
  265.0 5.2 %while.22 = (s32[]{:T(128)}, bf16[2,128,256]{2,1,0:T(8,128)(2,1)S(1)}, bf16[2,128,3584]{1,2,0:T(8,128)(2,1)}, bf16[128,28,256]{2,1,0:T(8,128)(2,1)}, f32[28,2]{1...) while((s32[]{:T(128)}, bf16[2,128,256]{2,1,0:T(8,128)(2,1)S(1)}, ...), condition=%wide.wide.region_8.9_spmd, body=%wide.wide.region_6.8_spmd.sunk | while | flops 236847104 | bytes 12439901 | solution.py:40
  270.9 7.7 %all-to-all-start.3 = ((bf16[2,128,256]{2,0,1:T(2,128)(2,1)}), bf16[2,128,256]{2,0,1:T(2,128)(2,1)S(1)}, u32[]{:S(2)}, u32[]{:S(2)}) async-start(bf16[2,128,256]{2,0,1:T(2,128)(2,1)} %copy.64), calls=%async_computation.3 | async-start | bytes 262144 | tf_op jit(solution)/shard_map/all_to_all | solution.py:41
  278.7 3.9 %reshape_reshape.8 = bf16[28,128,256]{2,1,0:T(8,128)(2,1)} reshape(bf16[128,28,256]{2,1,0:T(8,128)(2,1)} %get-tuple-element.307) | data formatting | bytes 3670016 | tf_op jit(solution)/shard_map/while/body/eval_jaxpr/reshape;reshape | solution.py:26
  282.6 4.6 %while.23 = (s32[]{:T(128)}, bf16[2,128,256]{2,1,0:T(8,128)(2,1)S(1)}, bf16[2,128,3584]{1,2,0:T(8,128)(2,1)S(1)}, bf16[128,28,256]{2,1,0:T(8,128)(2,1)}, f32[28,...) while((s32[]{:T(128)}, bf16[2,128,256]{2,1,0:T(8,128)(2,1)S(1)}, ...), condition=%wide.wide.region_16.17_spmd, body=%wide.wide.region_14.16_spmd.sunk | while | flops 236847104 | bytes 12439901 | solution.py:40
  288.0 3.0 all-to-all-done.3
  290.9 10.8 %all-to-all-start.5 = ((bf16[2,128,256]{2,0,1:T(2,128)(2,1)}), bf16[2,128,256]{2,0,1:T(2,128)(2,1)S(1)}, u32[]{:S(2)}, u32[]{:S(2)}) async-start(bf16[2,128,256]{2,0,1:T(2,128)(2,1)} %copy.72), calls=%async_computation.5 | async-start | bytes 262144 | tf_op jit(solution)/shard_map/all_to_all | solution.py:41
  301.9 3.7 %broadcast_in_dim_reshape.3 = bf16[1,3584,256]{2,1,0:T(8,128)(2,1)} reshape(bf16[128,28,256]{2,1,0:T(8,128)(2,1)} %get-tuple-element.308) | data formatting | bytes 3670016 | tf_op jit(solution)/shard_map/broadcast_in_dim;reshape | solution.py:95
  306.6 7.3 %all-to-all-done.5 = bf16[2,128,256]{2,0,1:T(2,128)(2,1)S(1)} async-done(((bf16[2,128,256]{2,0,1:T(2,128)(2,1)}), bf16[2,128,256]{2,0,1:T(2,128)(2,1)S(1)}, u32[]{:S(2)}, u32[]{:S(2)}) %all-to-all-start.5) | async-done | bytes 131104 | tf_op jit(solution)/shard_map/all_to_all | solution.py:41
  (85 shorter events, 26.3 us)
Async XLA Ops:
  0.6 212.8 %copy-start = (f32[128,28,2]{0,2,1:T(2,128)S(1)}, f32[128,28,2]{0,2,1:T(2,128)}, u32[]{:S(2)}) copy-start(f32[128,28,2]{0,2,1:T(2,128)} %param.15) | copy-start | bytes 86020
  20.7 67.0 %all-to-all-start = ((bf16[2,128,3584]{2,0,1:T(2,128)(2,1)}), bf16[2,128,3584]{2,0,1:T(2,128)(2,1)S(1)}, u32[]{:S(2)}, u32[]{:S(2)}) async-start(bf16[2,128,3584]{2,0,1:T(2,128)(2,1)} %copy.60), calls=%async_computation | async-start | bytes 3670016 | tf_op jit(solution)/shard_map/all_to_all | solution.py:89
  87.6 1.3 copy-start.3
  88.9 59.9 %all-to-all-start.1 = ((bf16[128,28,256]{2,1,0:T(8,128)(2,1)}), bf16[128,28,256]{2,1,0:T(8,128)(2,1)S(1)}, u32[]{:S(2)}, u32[]{:S(2)}) async-start(bf16[128,28,256]{2,1,0:T(8,128)(2,1)} %reshape_squeeze.3), calls=%async_computation.1 | async-start | bytes 4194304 | tf_op jit(solution)/shard_map/all_to_all | solution.py:68
  148.8 54.3 %all-to-all-start.4 = ((bf16[2,128,3584]{2,0,1:T(2,128)(2,1)}), bf16[2,128,3584]{2,0,1:T(2,128)(2,1)}, u32[]{:S(2)}, u32[]{:S(2)}) async-start(bf16[2,128,3584]{2,0,1:T(2,128)(2,1)} %copy.69), calls=%async_computation.4 | async-start | bytes 3670016 | tf_op jit(solution)/shard_map/all_to_all | solution.py:89
  162.2 48.7 %copy-start.7 = (s32[128]{0:T(128)S(1)}, s32[128]{0:T(128)}, u32[]{:S(2)}) copy-start(s32[128]{0:T(128)} %param.17) | copy-start | bytes 1540
  162.2 51.5 %copy-start.6 = (f32[2,16,8]{1,2,0:T(8,128)S(1)}, f32[2,16,8]{1,2,0:T(8,128)}, u32[]{:S(2)}) copy-start(f32[2,16,8]{1,2,0:T(8,128)} %param.13) | copy-start | bytes 3076
  203.1 59.9 %all-to-all-start.2 = ((bf16[128,28,256]{2,1,0:T(8,128)(2,1)}), bf16[128,28,256]{2,1,0:T(8,128)(2,1)S(1)}, u32[]{:S(2)}, u32[]{:S(2)}) async-start(bf16[128,28,256]{2,1,0:T(8,128)(2,1)} %broadcast_select_fusion), calls=%async_computation.2 | async-start | bytes 4194304 | tf_op jit(solution)/shard_map/all_to_all | solution.py:66
  263.1 1.9 copy-start.1
  265.0 1.8 copy-start.5
  267.6 1.8 copy-start.5
  270.9 20.0 %all-to-all-start.3 = ((bf16[2,128,256]{2,0,1:T(2,128)(2,1)}), bf16[2,128,256]{2,0,1:T(2,128)(2,1)S(1)}, u32[]{:S(2)}, u32[]{:S(2)}) async-start(bf16[2,128,256]{2,0,1:T(2,128)(2,1)} %copy.64), calls=%async_computation.3 | async-start | bytes 262144 | tf_op jit(solution)/shard_map/all_to_all | solution.py:41
  278.7 3.9 %copy-start.2 = (bf16[2,128,3584]{1,2,0:T(8,128)(2,1)S(1)}, bf16[2,128,3584]{1,2,0:T(8,128)(2,1)}, u32[]{:S(2)}) copy-start(bf16[2,128,3584]{1,2,0:T(8,128)(2,1)} %copy.70) | copy-start | bytes 5505028
  282.6 1.5 copy-start.4
  284.9 1.5 copy-start.4
  290.9 22.9 %all-to-all-start.5 = ((bf16[2,128,256]{2,0,1:T(2,128)(2,1)}), bf16[2,128,256]{2,0,1:T(2,128)(2,1)S(1)}, u32[]{:S(2)}, u32[]{:S(2)}) async-start(bf16[2,128,256]{2,0,1:T(2,128)(2,1)} %copy.72), calls=%async_computation.5 | async-start | bytes 262144 | tf_op jit(solution)/shard_map/all_to_all | solution.py:41
where the time goes:
time: 317 us; the launch traced here: 315 us
  waiting for transfers between devices  176 us (56%)
  starting transfers between devices  62.7 us (20%)
  local copies, waits for them, and re-layouts  54.2 us (17%)
  blocking collectives  10.5 us (3%)
  other arithmetic  5.92 us (2%)
    all_to_all x2, waiting for transfers between devices, shards(): lax.all_to_all(send_buffer, 'ep', split_axis=1, concat_axis=1, tiled=True)  83.6 us
    all_to_all x1, waiting for transfers between devices, shards(): lax.all_to_all(pieces, 'ep', split_axis=0, concat_axis=0, tiled=True)  44.2 us
    all_to_all x1, waiting for transfers between devices, shards(): lax.all_to_all(jnp.take(lax.all_to_all(pieces, 'ep', split_axis=0, concat...  38.2 us
    all_to_all x2, starting transfers between devices, shards(): lax.all_to_all(send_buffer, 'ep', split_axis=1, concat_axis=1, tiled=True)  28.6 us
    all_to_all x2, starting transfers between devices, serve_rows(): lax.all_to_all(activated, 'ep', split_axis=1, concat_axis=1, tiled=True)  18.5 us
    while x5, local copies, waits for them, and re-layouts, serve_rows(): activated = lax.map(one_slot, arrived)  12.7 us
    all_gather x1, blocking collectives, shards(): grouped = lax.all_gather(tokens, 'dp', axis=1, tiled=True)  10.5 us
    all_to_all x2, waiting for transfers between devices, serve_rows(): lax.all_to_all(activated, 'ep', split_axis=1, concat_axis=1, tiled=True)  10.3 us
  transfers between devices with their start and end apart: 6, of which 6 were waited for; matrix products, arithmetic and copies ran while one was open for 13% of the time, Pallas kernels for 0%

commit v1 on v0

--- a/solution.py
+++ b/solution.py
@@ -38,7 +38,12 @@
             return jax.nn.silu(scaled_product(slot_rows, weight_block, scales)).astype(jnp.bfloat16)
 
         activated = lax.map(one_slot, arrived)
-        return lax.all_to_all(activated, "ep", split_axis=1, concat_axis=1, tiled=True)
+        return jnp.concatenate(
+            lax.all_to_all(
+                jnp.stack(jnp.split(activated, lax.axis_size("ep"), axis=1)), "ep", 0, 0
+            ),
+            axis=1,
+        )
 
     return serve_rows
 

time: 317 us -> 463 us (1.46)
  local copies, waits for them, and re-layouts: 54.2 us -> 199 us
    unnamed x13 -> x267, local copies, waits for them, and re-layouts: 2.49 us -> 147 us
  transfers between devices with their start and end apart: 6 -> 6, of which waited for: 6 -> 5; matrix products, arithmetic and copies ran while one was open for 13% -> 24% of each run, Pallas kernels for 0% -> 0%
where the time goes in v1:
time: 463 us; the launch traced here: 461 us
  local copies, waits for them, and re-layouts  199 us (43%)
  waiting for transfers between devices  174 us (38%)
  starting transfers between devices  65.6 us (14%)
  blocking collectives  10.5 us (2%)
  other arithmetic  5.92 us (1%)
    unnamed x267, local copies, waits for them, and re-layouts  147 us
    all_to_all x2, waiting for transfers between devices, shards(): lax.all_to_all(send_buffer, 'ep', split_axis=1, concat_axis=1, tiled=True)  83.6 us
    all_to_all x1, waiting for transfers between devices, shards(): lax.all_to_all(pieces, 'ep', split_axis=0, concat_axis=0, tiled=True)  44.2 us
    all_to_all x1, waiting for transfers between devices, shards(): lax.all_to_all(jnp.take(lax.all_to_all(pieces, 'ep', split_axis=0, concat...  38.2 us
    all_to_all x2, starting transfers between devices, shards(): lax.all_to_all(send_buffer, 'ep', split_axis=1, concat_axis=1, tiled=True)  28.6 us
    all_to_all x2, starting transfers between devices, serve_rows(): lax.all_to_all(jnp.stack(jnp.split(activated, lax.axis_size('ep'), axis=1...  21.5 us
    while x5, local copies, waits for them, and re-layouts, serve_rows(): activated = lax.map(one_slot, arrived)  11.5 us
    all_gather x1, blocking collectives, shards(): grouped = lax.all_gather(tokens, 'dp', axis=1, tiled=True)  10.5 us
  transfers between devices with their start and end apart: 6, of which 5 were waited for; matrix products, arithmetic and copies ran while one was open for 24% of the time, Pallas kernels for 0%

profile of v1, /device:TPU:1, one launch (start us, length us, event | category | flops | bytes accessed | tf_op | source)
XLA Modules:
  0.0 461.4 jit_solution(8139449419542059061)
XLA Ops:
  3.1 10.5 %all_gather.3 = bf16[2,16,3584]{2,0,1:T(2,128)(2,1)S(1)} all-gather(bf16[2,4,3584]{2,0,1:T(2,128)(2,1)S(1)} %copy.1078), channel_id=1, replica_groups=mesh['ep'=128,'dp'=4] {'dp'}, dimensions={1}, use_global_device_ids=true | all-gather | bytes 286720 | tf_op jit(solution)/shard_map/all_gather | solution.py:82
  15.1 2.5 scatter_custom_fusion
  17.5 3.1 copy.1080
  20.7 20.5 %all-to-all-start = ((bf16[2,128,3584]{2,0,1:T(2,128)(2,1)}), bf16[2,128,3584]{2,0,1:T(2,128)(2,1)S(1)}, u32[]{:S(2)}, u32[]{:S(2)}) async-start(bf16[2,128,3584]{2,0,1:T(2,128)(2,1)} %copy.1080), calls=%async_computation | async-start | bytes 3670016 | tf_op jit(solution)/shard_map/all_to_all | solution.py:94
  41.1 3.7 reshape_squeeze.3
  44.9 42.7 %all-to-all-done = bf16[2,128,3584]{2,0,1:T(2,128)(2,1)S(1)} async-done(((bf16[2,128,3584]{2,0,1:T(2,128)(2,1)}), bf16[2,128,3584]{2,0,1:T(2,128)(2,1)S(1)}, u32[]{:S(2)}, u32[]{:S(2)}) %all-to-all-start) | async-done | bytes 1835040 | tf_op jit(solution)/shard_map/all_to_all | solution.py:94
  88.9 7.8 %all-to-all-start.1 = ((bf16[128,28,256]{2,1,0:T(8,128)(2,1)}), bf16[128,28,256]{2,1,0:T(8,128)(2,1)S(1)}, u32[]{:S(2)}, u32[]{:S(2)}) async-start(bf16[128,28,256]{2,1,0:T(8,128)(2,1)} %reshape_squeeze.3), calls=%async_computation.1 | async-start | bytes 4194304 | tf_op jit(solution)/shard_map/all_to_all | solution.py:73
  96.7 3.3 scatter_custom_fusion.1
  100.0 4.6 %copy.1215 = bf16[2,128,3584]{2,0,1:T(2,128)(2,1)} copy(bf16[2,128,3584]{2,1,0:T(8,128)(2,1)} %bitcast.1147) | data formatting | bytes 3670016 | tf_op jit(solution)/shard_map/reshape | solution.py:91
  104.6 44.2 %all-to-all-done.1 = bf16[128,28,256]{2,1,0:T(8,128)(2,1)S(1)} async-done(((bf16[128,28,256]{2,1,0:T(8,128)(2,1)}), bf16[128,28,256]{2,1,0:T(8,128)(2,1)S(1)}, u32[]{:S(2)}, u32[]{:S(2)}) %all-to-all-start.1) | async-done | bytes 1835040 | tf_op jit(solution)/shard_map/all_to_all | solution.py:73
  148.8 8.1 %all-to-all-start.4 = ((bf16[2,128,3584]{2,0,1:T(2,128)(2,1)}), bf16[2,128,3584]{2,0,1:T(2,128)(2,1)}, u32[]{:S(2)}, u32[]{:S(2)}) async-start(bf16[2,128,3584]{2,0,1:T(2,128)(2,1)} %copy.1215), calls=%async_computation.4 | async-start | bytes 3670016 | tf_op jit(solution)/shard_map/all_to_all | solution.py:94
  159.0 3.2 broadcast_select_fusion
  162.2 40.9 %all-to-all-done.4 = bf16[2,128,3584]{2,0,1:T(2,128)(2,1)} async-done(((bf16[2,128,3584]{2,0,1:T(2,128)(2,1)}), bf16[2,128,3584]{2,0,1:T(2,128)(2,1)}, u32[]{:S(2)}, u32[]{:S(2)}) %all-to-all-start.4) | async-done | bytes 1835040 | tf_op jit(solution)/shard_map/all_to_all | solution.py:94
  203.1 7.8 %all-to-all-start.2 = ((bf16[128,28,256]{2,1,0:T(8,128)(2,1)}), bf16[128,28,256]{2,1,0:T(8,128)(2,1)S(1)}, u32[]{:S(2)}, u32[]{:S(2)}) async-start(bf16[128,28,256]{2,1,0:T(8,128)(2,1)} %broadcast_select_fusion), calls=%async_computation.2 | async-start | bytes 4194304 | tf_op jit(solution)/shard_map/all_to_all | solution.py:71
  213.8 5.5 %copy.1082 = bf16[2,128,3584]{1,2,0:T(8,128)(2,1)} copy(bf16[2,128,3584]{2,0,1:T(2,128)(2,1)} %copy-done.3) | data formatting | bytes 3670016 | tf_op jit(solution)/shard_map/while | solution.py:40
  219.3 5.5 %copy.1216 = bf16[2,128,3584]{1,2,0:T(8,128)(2,1)} copy(bf16[2,128,3584]{2,0,1:T(2,128)(2,1)} %all-to-all-done.4) | data formatting | bytes 3670016 | tf_op jit(solution)/shard_map/while | solution.py:40
  224.9 38.2 %all-to-all-done.2 = bf16[128,28,256]{2,1,0:T(8,128)(2,1)S(1)} async-done(((bf16[128,28,256]{2,1,0:T(8,128)(2,1)}), bf16[128,28,256]{2,1,0:T(8,128)(2,1)S(1)}, u32[]{:S(2)}, u32[]{:S(2)}) %all-to-all-start.2) | async-done | bytes 1835040 | tf_op jit(solution)/shard_map/all_to_all | solution.py:71
  265.0 5.2 %while.22 = (s32[]{:T(128)}, bf16[2,128,256]{2,1,0:T(8,128)(2,1)S(1)}, bf16[2,128,3584]{1,2,0:T(8,128)(2,1)}, bf16[128,28,256]{2,1,0:T(8,128)(2,1)}, f32[28,2]{1...) while((s32[]{:T(128)}, bf16[2,128,256]{2,1,0:T(8,128)(2,1)S(1)}, ...), condition=%wide.wide.region_8.9_spmd, body=%wide.wide.region_6.8_spmd.sunk | while | flops 236847104 | bytes 12439901 | solution.py:40
  343.2 7.7 %all-to-all-start.3 = ((bf16[128,2,1,256]{3,1,2,0:T(2,128)(2,1)}), bf16[128,2,1,256]{3,1,2,0:T(2,128)(2,1)S(1)}, u32[]{:S(2)}, u32[]{:S(2)}) async-start(bf16[128,2,1,256]{3,1,2,0:T(2,128)(2,1)} %constant_dynamic-update-slice_fusion), calls=%async_computation.3 | async-start | bytes 262144 | tf_op jit(solution)/shard_map/all_to_all | solution.py:42
  350.9 3.9 reshape_reshape.16
  354.8 4.6 while.23
  432.9 13.7 %all-to-all-start.5 = ((bf16[128,2,1,256]{3,1,2,0:T(2,128)(2,1)}), bf16[128,2,1,256]{3,1,2,0:T(2,128)(2,1)S(1)}, u32[]{:S(2)}, u32[]{:S(2)}) async-start(bf16[128,2,1,256]{3,1,2,0:T(2,128)(2,1)} %constant_dynamic-update-slice_fusion.128), calls=%async_computation.5 | async-start | bytes 262144 | tf_op jit(solution)/shard_map/all_to_all | solution.py:42
  446.8 3.7 broadcast_in_dim_reshape.3
  450.6 8.2 %all-to-all-done.5 = bf16[128,2,1,256]{3,1,2,0:T(2,128)(2,1)S(1)} async-done(((bf16[128,2,1,256]{3,1,2,0:T(2,128)(2,1)}), bf16[128,2,1,256]{3,1,2,0:T(2,128)(2,1)S(1)}, u32[]{:S(2)}, u32[]{:S(2)}) %all-to-all-start.5) | async-done | bytes 131104 | tf_op jit(solution)/shard_map/all_to_all | solution.py:42
  (343 shorter events, 168.6 us)
Async XLA Ops:
  0.6 212.8 %copy-start = (f32[128,28,2]{0,2,1:T(2,128)S(1)}, f32[128,28,2]{0,2,1:T(2,128)}, u32[]{:S(2)}) copy-start(f32[128,28,2]{0,2,1:T(2,128)} %param.15) | copy-start | bytes 86020
  20.7 67.0 %all-to-all-start = ((bf16[2,128,3584]{2,0,1:T(2,128)(2,1)}), bf16[2,128,3584]{2,0,1:T(2,128)(2,1)S(1)}, u32[]{:S(2)}, u32[]{:S(2)}) async-start(bf16[2,128,3584]{2,0,1:T(2,128)(2,1)} %copy.1080), calls=%async_computation | async-start | bytes 3670016 | tf_op jit(solution)/shard_map/all_to_all | solution.py:94
  87.6 1.3 copy-start.3
  88.9 59.9 %all-to-all-start.1 = ((bf16[128,28,256]{2,1,0:T(8,128)(2,1)}), bf16[128,28,256]{2,1,0:T(8,128)(2,1)S(1)}, u32[]{:S(2)}, u32[]{:S(2)}) async-start(bf16[128,28,256]{2,1,0:T(8,128)(2,1)} %reshape_squeeze.3), calls=%async_computation.1 | async-start | bytes 4194304 | tf_op jit(solution)/shard_map/all_to_all | solution.py:73
  148.8 54.3 %all-to-all-start.4 = ((bf16[2,128,3584]{2,0,1:T(2,128)(2,1)}), bf16[2,128,3584]{2,0,1:T(2,128)(2,1)}, u32[]{:S(2)}, u32[]{:S(2)}) async-start(bf16[2,128,3584]{2,0,1:T(2,128)(2,1)} %copy.1215), calls=%async_computation.4 | async-start | bytes 3670016 | tf_op jit(solution)/shard_map/all_to_all | solution.py:94
  162.2 48.7 %copy-start.7 = (s32[128]{0:T(128)S(1)}, s32[128]{0:T(128)}, u32[]{:S(2)}) copy-start(s32[128]{0:T(128)} %param.17) | copy-start | bytes 1540
  203.1 59.9 %all-to-all-start.2 = ((bf16[128,28,256]{2,1,0:T(8,128)(2,1)}), bf16[128,28,256]{2,1,0:T(8,128)(2,1)S(1)}, u32[]{:S(2)}, u32[]{:S(2)}) async-start(bf16[128,28,256]{2,1,0:T(8,128)(2,1)} %broadcast_select_fusion), calls=%async_computation.2 | async-start | bytes 4194304 | tf_op jit(solution)/shard_map/all_to_all | solution.py:71
  263.1 1.9 copy-start.1
  265.0 1.8 copy-start.5
  267.6 1.8 copy-start.5
  343.2 89.7 %all-to-all-start.3 = ((bf16[128,2,1,256]{3,1,2,0:T(2,128)(2,1)}), bf16[128,2,1,256]{3,1,2,0:T(2,128)(2,1)S(1)}, u32[]{:S(2)}, u32[]{:S(2)}) async-start(bf16[128,2,1,256]{3,1,2,0:T(2,128)(2,1)} %constant_dynamic-update-slice_fusion), calls=%async_computation.3 | async-start | bytes 262144 | tf_op jit(solution)/shard_map/all_to_all | solution.py:42
  350.9 3.9 copy-start.2
  354.8 91.8 %copy-start.6 = (f32[2,16,8]{1,2,0:T(8,128)S(1)}, f32[2,16,8]{1,2,0:T(8,128)}, u32[]{:S(2)}) copy-start(f32[2,16,8]{1,2,0:T(8,128)} %param.13) | copy-start | bytes 3076
  354.8 1.5 copy-start.4
  357.1 1.5 copy-start.4
  432.9 25.9 %all-to-all-start.5 = ((bf16[128,2,1,256]{3,1,2,0:T(2,128)(2,1)}), bf16[128,2,1,256]{3,1,2,0:T(2,128)(2,1)S(1)}, u32[]{:S(2)}, u32[]{:S(2)}) async-start(bf16[128,2,1,256]{3,1,2,0:T(2,128)(2,1)} %constant_dynamic-update-slice_fusion.128), calls=%async_computation.5 | async-start | bytes 262144 | tf_op jit(solution)/shard_map/all_to_all | solution.py:42
